TPU v7x, 128 devices: a whole 4x4x4 slice. The times are simulated.
128 devices in a mesh: dp: 8 (over x_hi, z), tensor: 16 (over y, x_lo, core).
Axes of the slice: x: 4 (x_hi: 2, x_lo: 2; x = x_hi * 2 + x_lo), y: 4, z: 4, core: 2. Of those that a mesh axis runs over, the one named last changes fastest.
Arguments:
- tokens: bfloat16 [16384, 2048], P(('dp', 'tensor')), parts along dimension 0, may hold values from -6 to 6
- segment_ids: int32 [16384], P('dp'), parts along dimension 0, may hold values from 0 to 3, never falling along the last dimension, each value on 1 to 1024 neighbouring positions
- attention_gain: float32 [2048], replicated, may hold values from 0.1 to 1.9
- query_weight: bfloat16 [2048, 2048], P(None, 'tensor'), may hold values from -1 to 1
- key_weight: bfloat16 [2048, 2048], P(None, 'tensor'), may hold values from -1 to 1
- value_weight: bfloat16 [2048, 2048], P(None, 'tensor'), may hold values from -0.125 to 0.125
- output_weight: bfloat16 [2048, 2048], P('tensor'), may hold values from -0.125 to 0.125
- ffn_gain: float32 [2048], replicated, may hold values from 0.1 to 1.9
- shared_gate: bfloat16 [2048, 2816], P(None, 'tensor'), may hold values from -0.125 to 0.125
- shared_up: bfloat16 [2048, 2816], P(None, 'tensor'), may hold values from -0.125 to 0.125
- shared_down: bfloat16 [2816, 2048], P('tensor'), may hold values from -0.109375 to 0.109375
- expert_gate: bfloat16 [16, 2048, 1408], P('tensor'), may hold values from -0.125 to 0.125
- expert_up: bfloat16 [16, 2048, 1408], P('tensor'), may hold values from -0.125 to 0.125
- expert_down: bfloat16 [16, 1408, 2048], P('tensor'), may hold values from -0.15625 to 0.15625
- expert_ids: int32 [16384, 6], P('dp'), parts along dimension 0, may hold values from 0 to 15, all different within a row; in each aligned block of 128 rows (0 to 127, 128 to 255, ...) at most 64 rows name the same one
- gate_weights: float32 [16384, 6], P('dp'), parts along dimension 0, may hold values from 0.05 to 0.35
- page_table: int32 [128], P('dp'), parts along dimension 0, may hold values from 0 to 15, each once
Outputs:
- layer_out: bfloat16 [16384, 2048], P(('dp', 'tensor')), parts along dimension 0
- kv_pages: bfloat16 [2, 128, 128, 2048], P(None, 'dp', None, 'tensor'), parts along dimension 1
There are 8 independent parts, one for each index of `dp`. A program takes and returns all parts, laid end to end along the dimension named above; an argument that names none is the same for every part. Nothing has to cross between parts.
Inputs may be any that keep to these rules, and one draw needn't show every extreme that they name: `segment_ids`: ids never fall along the stream; each of the 4 prompts holds 1 to 1024 tokens and one holds exactly 1024. `expert_ids`: each row names 6 different experts; within each aligned block of 128 rows (the tokens of one index of tensor) no expert is named by more than 64 rows, a bound that some block reaches. `page_table`: each cache page is named once.
All inputs are finite; a program needn't handle non-finite values.
Results may differ from a plain program's by a relative error of at most 0.02.
The roundings to bfloat16 on the way count: a program that leaves them out, or rounds other values in their place, can miss the bound.
Values may be sent and summed in bfloat16 or wider, within the bound.
No kernel may reach another device: no remote copies, remote signals or barrier semaphores. Data moves between devices by JAX's collectives and lax.ppermute only.
A program may use at most 128 MiB of HBM per device.

v0:
```python
import jax
import jax.numpy as jnp
from jax import lax
from jax.sharding import PartitionSpec as P

HD = 128
TOP = 6
PAGE = 128


def rms_scale(hidden, gain):
    widened = hidden.astype(jnp.float32)
    inverse = lax.rsqrt(jnp.mean(widened * widened, axis=-1, keepdims=True) + 1e-06)
    return (widened * inverse * gain).astype(jnp.bfloat16)


def attend(projected, segment_ids, head_count):
    total_tokens = projected.shape[0]
    inner = head_count * HD
    queries = projected[:, :inner].reshape(total_tokens, head_count, HD)
    keys = projected[:, inner : 2 * inner].reshape(total_tokens, head_count, HD)
    values = projected[:, 2 * inner :].reshape(total_tokens, head_count, HD)
    scale = HD ** (-0.5)
    positions = jnp.arange(total_tokens, dtype=jnp.int32)
    span = min(512, total_tokens)

    def one_block(start):
        query_rows = lax.dynamic_slice_in_dim(queries, start, span, 0)
        query_segments = lax.dynamic_slice_in_dim(segment_ids, start, span, 0)
        query_positions = start + jnp.arange(span, dtype=jnp.int32)
        scores = (
            jnp.einsum("qhd,khd->hqk", query_rows, keys, preferred_element_type=jnp.float32) * scale
        )
        allowed = (query_segments[:, None] == segment_ids[None, :]) & (
            positions[None, :] <= query_positions[:, None]
        )
        scores = jnp.where(allowed[None], scores, -jnp.inf)
        highest = jnp.max(scores, axis=-1, keepdims=True)
        weights = jnp.exp(scores - highest)
        probs = (weights / jnp.sum(weights, axis=-1, keepdims=True)).astype(jnp.bfloat16)
        context = jnp.einsum("hqk,khd->qhd", probs, values, preferred_element_type=jnp.float32)
        return context.astype(jnp.bfloat16)

    starts = jnp.arange(total_tokens // span, dtype=jnp.int32) * span
    context = lax.map(one_block, starts).reshape(total_tokens, inner)
    return (context, keys.reshape(total_tokens, inner), values.reshape(total_tokens, inner))


def slot_tables(block_ids, block_gates, expert_count, capacity):
    row_count = block_ids.shape[0]
    labels = jnp.arange(expert_count, dtype=jnp.int32)
    match = (block_ids[:, :, None] == labels[None, None, :]).astype(jnp.int32)
    hits = jnp.sum(match, axis=1)
    before = jnp.cumsum(hits, axis=0) - hits
    rank = jnp.sum(match * before[:, None, :], axis=2)
    flat = (block_ids * capacity + rank).reshape(-1)
    owner = jnp.broadcast_to(jnp.arange(row_count, dtype=jnp.int32)[:, None], block_ids.shape)
    slot_token = jnp.zeros((expert_count * capacity,), jnp.int32).at[flat].set(owner.reshape(-1))
    slot_weight = (
        jnp.zeros((expert_count * capacity,), jnp.float32).at[flat].set(block_gates.reshape(-1))
    )
    return (slot_token, slot_weight)


def expert_apply(incoming, expert_gate, expert_up, expert_down):
    gate_part = jnp.einsum(
        "secd,edf->secf", incoming, expert_gate, preferred_element_type=jnp.float32
    )
    upward = jnp.einsum("secd,edf->secf", incoming, expert_up, preferred_element_type=jnp.float32)
    hidden = (jax.nn.silu(gate_part) * upward).astype(jnp.bfloat16)
    produced = jnp.einsum("secf,efd->secd", hidden, expert_down, preferred_element_type=jnp.float32)
    return produced.astype(jnp.bfloat16)


def shards(
    tokens,
    segment_ids,
    attention_gain,
    query_weight,
    key_weight,
    value_weight,
    output_weight,
    ffn_gain,
    shared_gate,
    shared_up,
    shared_down,
    expert_gate,
    expert_up,
    expert_down,
    expert_ids,
    gate_weights,
    page_table,
):
    tok_dev = tokens.shape[0]
    groups = lax.axis_size("tensor")
    position = lax.axis_index("tensor")
    inner = query_weight.shape[1]
    head_count = inner // HD
    projection = jnp.concatenate([query_weight, key_weight, value_weight], axis=1)
    projected = jnp.dot(
        rms_scale(lax.all_gather(tokens, "tensor", axis=0, tiled=True), attention_gain),
        projection,
        preferred_element_type=jnp.float32,
    ).astype(jnp.bfloat16)
    context, keys, values = attend(projected, segment_ids, head_count)
    cache = jnp.stack([keys, values]).reshape(2, -1, PAGE, inner)
    kv_pages = jnp.zeros_like(cache).at[:, page_table].set(cache)
    attention = lax.psum_scatter(
        jnp.dot(context, output_weight, preferred_element_type=jnp.float32).astype(jnp.bfloat16),
        "tensor",
        scatter_dimension=0,
        tiled=True,
    ).astype(jnp.float32)
    residual = (tokens.astype(jnp.float32) + attention).astype(jnp.bfloat16)
    normed_ffn = rms_scale(residual, ffn_gain)
    shared_columns = jnp.concatenate([shared_gate, shared_up], axis=1)
    shared_width = shared_gate.shape[1]
    local_experts = expert_gate.shape[0]
    expert_count = local_experts * groups
    capacity = tok_dev * TOP // expert_count + tok_dev // 8
    id_blocks = expert_ids.reshape(groups, tok_dev, -1)
    gate_blocks = gate_weights.reshape(groups, tok_dev, -1)

    def block_table(id_block, gate_block):
        return slot_tables(id_block, gate_block, expert_count, capacity)

    all_tokens, all_weights = jax.vmap(block_table)(id_blocks, gate_blocks)
    all_tokens = all_tokens.reshape(groups, expert_count, capacity)
    all_weights = all_weights.reshape(groups, expert_count, capacity)
    chosen_slots = lax.dynamic_slice_in_dim(all_tokens, position * local_experts, local_experts, 1)
    chosen_weights = lax.dynamic_slice_in_dim(
        all_weights, position * local_experts, local_experts, 1
    )
    offsets = (jnp.arange(groups, dtype=jnp.int32) * tok_dev)[:, None, None]
    stream_slots = (chosen_slots + offsets).reshape(-1)
    joined = jnp.dot(
        lax.all_gather(normed_ffn, "tensor", axis=0, tiled=True),
        shared_columns,
        preferred_element_type=jnp.float32,
    )
    hidden_all = (jax.nn.silu(joined[:, :shared_width]) * joined[:, shared_width:]).astype(
        jnp.bfloat16
    )
    own_slots = all_tokens[position]
    outgoing = normed_ffn[own_slots.reshape(-1)].reshape(groups, local_experts, capacity, -1)
    produced = expert_apply(
        lax.all_to_all(outgoing, "tensor", split_axis=0, concat_axis=0, tiled=True),
        expert_gate,
        expert_up,
        expert_down,
    )
    term = jnp.dot(hidden_all, shared_down, preferred_element_type=jnp.float32)
    model_width = term.shape[1]
    weighted = chosen_weights.reshape(-1, 1) * produced.reshape(-1, model_width).astype(jnp.float32)
    term = term.at[stream_slots].add(weighted)
    ffn_out = lax.psum_scatter(
        term.astype(jnp.bfloat16), "tensor", scatter_dimension=0, tiled=True
    ).astype(jnp.float32)
    layer_out = (residual.astype(jnp.float32) + ffn_out).astype(jnp.bfloat16)
    return (layer_out, kv_pages)


def solution(mesh):
    placed = (
        P(("dp", "tensor"), None),
        P("dp"),
        P(),
        P(None, "tensor"),
        P(None, "tensor"),
        P(None, "tensor"),
        P("tensor", None),
        P(),
        P(None, "tensor"),
        P(None, "tensor"),
        P("tensor", None),
        P("tensor", None, None),
        P("tensor", None, None),
        P("tensor", None, None),
        P("dp", None),
        P("dp", None),
        P("dp"),
    )
    return jax.shard_map(
        shards,
        mesh=mesh,
        in_specs=placed,
        out_specs=(P(("dp", "tensor"), None), P(None, "dp", None, "tensor")),
        check_vma=False,
    )
```

profile of v0, /device:TPU:0, one launch (start us, length us, event | category | flops | bytes accessed | tf_op | source)
XLA Modules:
  0.0 538.0 jit_solution(10992776695320439391)
XLA Ops:
  7.2 0.7 all-gather.3.cloned.1.call-update
  8.0 56.3 %all-gather.3.cloned.1.call-done = bf16[2048,2048]{1,0:T(8,128)(2,1)} async-done(((bf16[128,2048]{1,0:T(8,128)(2,1)}), bf16[2048,2048]{1,0:T(8,128)(2,1)}) %all-gather.3.cloned.1.call-update) | async-done | bytes 8388624 | tf_op jit(solution)/shard_map/all_gather | solution.py:101
  64.3 5.2 fusion.13
  70.1 6.0 %fusion.44 = bf16[2048,384]{1,0:T(8,128)(2,1)S(1)} fusion(bf16[2048,2048]{1,0:T(8,128)(2,1)S(1)} %copy-done.2, f32[2048]{0:T(1024)S(1)} %copy-done.13, f32[2048]{0:T(1024)S(1)} %add_rsqrt_fusion, bf16[2048,128]{1,0:T(8,128)(2,1)S(1)} %copy-done.12, bf16[2048,128]{1,0:T(8,128)(2,1)} %param.23, bf16[2048,128]{1,0:T(8,128)(2,1)} %param.22), kind=kOutput, calls=%fused_computation.51 | convolution fusion | flops 3243507712 | bytes 11550720 | tf_op jit(solution)/shard_map/dot_general | solution.py:100
  76.1 1.2 fusion.77
  77.3 25.8 %while.11 = (s32[]{:T(128)}, bf16[4,512,1,128]{3,1,2,0:T(8,128)(2,1)S(1)}, s32[4]{0:T(128)S(1)}, s32[2048]{0:T(1024)S(1)}, bf16[2048,1,128]{2,0,1:T(8,128)(2,1)S...) while((s32[]{:T(128)}, ...), condition=%wide.region_4.5_spmd.clone, body=%wide.region_1.4_spmd.clone.sunk | while | flops 548470272 | bytes 13922475 | solution.py:45
  80.0 0.7 iota_add_fusion.2
  80.8 1.3 fusion.89
  82.0 0.7 fusion.90
  82.8 0.9 fusion.91
  86.4 0.7 iota_add_fusion.2
  87.2 1.3 fusion.89
  88.5 0.7 fusion.90
  89.2 0.9 fusion.91
  92.9 0.7 iota_add_fusion.2
  93.7 1.3 fusion.89
  94.9 0.7 fusion.90
  95.6 0.9 fusion.91
  99.3 0.7 iota_add_fusion.2
  100.1 1.3 fusion.89
  101.4 0.7 fusion.90
  102.1 0.9 fusion.91
  103.0 6.6 %convolution_convert_fusion = bf16[2048,2048]{1,0:T(8,128)(2,1)} fusion(bf16[2048,128]{1,0:T(8,128)(2,1)S(1)} %bitcast.144, bf16[128,2048]{1,0:T(8,128)(2,1)} %param.25), kind=kOutput, calls=%fused_computation.32 | convolution fusion | flops 1077936128 | bytes 9437184 | tf_op jit(solution)/shard_map/dot_general | solution.py:109
  110.2 98.4 %reduce-scatter.3.cloned.1.call-done = bf16[128,2048]{1,0:T(8,128)(2,1)} async-done(((bf16[2048,2048]{1,0:T(8,128)(2,1)}), bf16[128,2048]{1,0:T(8,128)(2,1)}) %reduce-scatter.3.cloned.1.call-update) | async-done | bytes 524304 | tf_op jit(solution)/shard_map/reduce_scatter | solution.py:108
  208.6 1.3 fusion.61
  209.9 2.0 fusion.63
  212.7 1.3 copy.41
  214.1 1.7 mul.116
  215.8 23.3 %fusion.78 = s32[16,128,16]{2,0,1:T(8,128)S(1)} fusion(s32[16,128,16]{2,0,1:T(8,128)S(1)} %copy.43), kind=kOutput, calls=%fused_computation.107 | output fusion | flops 4161536 | bytes 262144 | tf_op jit(solution)/shard_map/vmap(jit(cumsum))/reduce_window_sum | solution.py:54
  239.1 1.1 sub.16
  240.2 1.6 copy.45
  242.7 45.4 %scatter_custom_fusion.2 = s32[16384]{0:T(1024)S(1)} fusion(s32[12288]{0:T(1024)S(1)} %reshape.275, s32[12288]{0:T(1024)S(1)} %reshape.277, s32[]{:T(128)} %constant.27.clone.1), kind=kCustom, calls=%fused_computation.84 | custom fusion | bytes 65540
  288.4 6.1 %gather_fusion = bf16[1024,2048]{1,0:T(8,128)(2,1)} fusion(bf16[128,2048]{1,0:T(8,128)(2,1)S(1)} %copy-done.1, s32[1024]{0:T(1024)S(1)} %broadcast_clamp_fusion), kind=kCustom, calls=%fused_computation | custom fusion | bytes 8392704 | tf_op jit(solution)/shard_map/gather | solution.py:145
  294.4 4.7 all-to-all-start
  299.7 0.7 reshape.283
  300.4 45.6 %scatter_custom_fusion.3 = f32[16384]{0:T(1024)S(1)} fusion(s32[12288]{0:T(1024)S(1)} %reshape.275, f32[12288]{0:T(1024)S(1)} %reshape.283, f32[]{:T(128)} %constant.9.clone.1), kind=kCustom, calls=%fused_computation.82 | custom fusion | bytes 65540
  346.2 3.3 all-to-all-done
  349.5 11.7 %fusion.24 = f32[16,64,1408]{2,1,0:T(8,128)} fusion(bf16[1,2048,1408]{2,1,0:T(8,128)(2,1)} %param.31, bf16[16,1,64,2048]{3,2,1,0:T(8,128)(2,1)} %all-to-all-done), kind=kOutput, calls=%fused_computation.37 | convolution fusion | flops 5905580032 | bytes 15728640 | tf_op jit(solution)/shard_map/secd,edf->secf/dot_general | solution.py:69
  361.2 21.0 %fusion.36 = bf16[16,64,2048]{2,1,0:T(8,128)(2,1)} fusion(bf16[1,1408,2048]{2,1,0:T(8,128)(2,1)} %param.32, f32[16,64,1408]{2,1,0:T(8,128)} %fusion.24, bf16[1,2048,1408]{2,1,0:T(8,128)(2,1)} %param.30, bf16[16,1,64,2048]{3,2,1,0:T(8,128)(2,1)} %all-to-all-done), kind=kOutput, calls=%fused_computation.49 | convolution fusion | flops 11821907968 | bytes 25690112 | tf_op jit(solution)/shard_map/secf,efd->secd/dot_general | solution.py:71
  382.2 5.8 %fusion.57 = f32[2048,352]{0,1:T(8,128)S(1)} fusion(bf16[2048,2048]{1,0:T(8,128)(2,1)} %all-gather.5.cloned.1.call-done, bf16[2048,176]{0,1:T(8,128)(2,1)S(1)} %copy-done.11, bf16[2048,176]{0,1:T(8,128)(2,1)} %param.27), kind=kOutput, calls=%fused_computation.62 | convolution fusion | flops 2955673600 | bytes 12713984 | tf_op jit(solution)/shard_map/dot_general | solution.py:136
  388.0 8.1 %fusion.65 = f32[2048,2048]{1,0:T(8,128)} fusion(bf16[176,2048]{1,0:T(8,128)(2,1)S(1)} %copy-done, f32[2048,352]{0,1:T(8,128)S(1)} %fusion.57), kind=kOutput, calls=%fused_computation.75 | convolution fusion | flops 1478557696 | bytes 20381696 | tf_op jit(solution)/shard_map/dot_general | solution.py:152
  396.1 26.5 %scatter_custom_fusion = f32[2048,2048]{1,0:T(8,128)} fusion(f32[2048,2048]{1,0:T(8,128)} %fusion.65, s32[1024]{0:T(1024)S(1)} %bitcast.148, bf16[1024,2048]{1,0:T(8,128)(2,1)} %bitcast.141, f32[1024]{0:T(1024)S(1)} %mul.120), kind=kCustom, calls=%fused_computation.29 | custom fusion | flops 6291456 | bytes 20975616 | tf_op jit(solution)/shard_map/scatter-add | solution.py:155
  422.7 9.1 %convert_element_type.101 = bf16[2048,2048]{1,0:T(8,128)(2,1)} convert(f32[2048,2048]{1,0:T(8,128)} %scatter_custom_fusion) | non-fusion elementwise | flops 4194304 | bytes 25165824 | tf_op jit(solution)/shard_map/convert_element_type | solution.py:157
  432.4 1.2 maximum_bitcast_fusion
  433.6 1.2 broadcast_in_dim.34
  434.8 3.0 scatter_fusion
  437.8 91.4 %reduce-scatter.5.cloned.1.call-done = bf16[128,2048]{1,0:T(8,128)(2,1)} async-done(((bf16[2048,2048]{1,0:T(8,128)(2,1)}), bf16[128,2048]{1,0:T(8,128)(2,1)}) %reduce-scatter.5.cloned.1.call-update) | async-done | bytes 524304 | tf_op jit(solution)/shard_map/reduce_scatter | solution.py:156
  529.2 2.1 fusion.64
  (81 shorter events, 7.4 us)
Async XLA Ops:
  7.2 380.8 %copy-start = (bf16[176,2048]{1,0:T(8,128)(2,1)S(1)}, bf16[176,2048]{1,0:T(8,128)(2,1)}, u32[]{:S(2)}) copy-start(bf16[176,2048]{1,0:T(8,128)(2,1)} %param.29) | copy-start | bytes 2162692
  7.2 57.1 %all-gather.3.cloned.1.call-start = ((), (), s32[]{:S(2)}) async-start(), calls=%async_computation.3 | async-start | bytes 8912896 | tf_op jit(solution)/shard_map/all_gather | solution.py:101
  7.2 62.3 %copy-start.12 = (bf16[2048,128]{1,0:T(8,128)(2,1)S(1)}, bf16[2048,128]{1,0:T(8,128)(2,1)}, u32[]{:S(2)}) copy-start(bf16[2048,128]{1,0:T(8,128)(2,1)} %param.24) | copy-start | bytes 1572868
  7.9 200.7 %reduce-scatter.3.cloned.1.call-start = ((), (), s32[]{:S(2)}) async-start(), calls=%async_computation.4 | async-start | bytes 8912896 | tf_op jit(solution)/shard_map/reduce_scatter | solution.py:108
  8.0 61.6 %copy-start.13 = (f32[2048]{0:T(1024)S(1)}, f32[2048]{0:T(1024)}, u32[]{:S(2)}) copy-start(f32[2048]{0:T(1024)} %param.21) | copy-start | bytes 24580
  64.3 5.8 %copy-start.2 = (bf16[2048,2048]{1,0:T(8,128)(2,1)S(1)}, bf16[2048,2048]{1,0:T(8,128)(2,1)}, u32[]{:S(2)}) copy-start(bf16[2048,2048]{1,0:T(8,128)(2,1)} %all-gather.3.cloned.1.call-done) | copy-start | bytes 25165828
  76.1 1.2 copy-start.7
  109.6 98.9 %copy-start.3 = (bf16[128,2048]{1,0:T(8,128)(2,1)S(1)}, bf16[128,2048]{1,0:T(8,128)(2,1)}, u32[]{:S(2)}) copy-start(bf16[128,2048]{1,0:T(8,128)(2,1)} %param.19) | copy-start | bytes 1572868
  109.6 100.3 %copy-start.8 = (f32[2048]{0:T(1024)S(1)}, f32[2048]{0:T(1024)}, u32[]{:S(2)}) copy-start(f32[2048]{0:T(1024)} %param.26) | copy-start | bytes 24580
  109.6 102.5 %copy-start.5 = (s32[2048,6]{0,1:T(8,128)S(1)}, s32[2048,6]{0,1:T(8,128)}, u32[]{:S(2)}) copy-start(s32[2048,6]{0,1:T(8,128)} %param.33) | copy-start | bytes 147460
  109.7 272.5 %all-gather.5.cloned.1.call-start = ((), (), s32[]{:S(2)}) async-start(), calls=%async_computation.5 | async-start | bytes 8912896 | tf_op jit(solution)/shard_map/all_gather | solution.py:137
  215.8 26.8 %copy-start.10 = (s32[2]{0:T(128)S(1)}, s32[2]{0:T(128)}, u32[]{:S(2)}) copy-start(s32[2]{0:T(128)} %constant.41) | copy-start | bytes 28
  215.8 26.8 %copy-start.9 = (s32[2]{0:T(128)S(1)}, s32[2]{0:T(128)}, u32[]{:S(2)}) copy-start(s32[2]{0:T(128)} %constant.69) | copy-start | bytes 28
  239.1 49.3 %copy-start.1 = (bf16[128,2048]{1,0:T(8,128)(2,1)S(1)}, bf16[128,2048]{1,0:T(8,128)(2,1)}, u32[]{:S(2)}) copy-start(bf16[128,2048]{1,0:T(8,128)(2,1)} %fusion.63) | copy-start | bytes 1572868
  294.4 4.9 copy-start.6
  294.4 55.0 %all-to-all-start = ((bf16[16,1,64,2048]{3,2,1,0:T(8,128)(2,1)}), bf16[16,1,64,2048]{3,2,1,0:T(8,128)(2,1)}, u32[]{:S(2)}, u32[]{:S(2)}) async-start(bf16[16,1,64,2048]{3,2,1,0:T(8,128)(2,1)} %bitcast.140), calls=%async_computation.1 | async-start | bytes 8388608 | tf_op jit(solution)/shard_map/all_to_all | solution.py:147
  299.1 230.1 %reduce-scatter.5.cloned.1.call-start = ((), (), s32[]{:S(2)}) async-start(), calls=%async_computation.6 | async-start | bytes 8912896 | tf_op jit(solution)/shard_map/reduce_scatter | solution.py:156
  361.2 21.0 %copy-start.11 = (bf16[2048,176]{0,1:T(8,128)(2,1)S(1)}, bf16[2048,176]{0,1:T(8,128)(2,1)}, u32[]{:S(2)}) copy-start(bf16[2048,176]{0,1:T(8,128)(2,1)} %param.28) | copy-start | bytes 2162692
  431.7 0.7 copy-start.14
  432.4 96.8 %copy-start.4 = (bf16[128,2048]{1,0:T(8,128)(2,1)S(1)}, bf16[128,2048]{1,0:T(8,128)(2,1)}, u32[]{:S(2)}) copy-start(bf16[128,2048]{1,0:T(8,128)(2,1)} %reduce-scatter.3.cloned.1.call-done) | copy-start | bytes 1572868
Sparse Core Ops, SparseCore 0:
  9.7 54.5 all-gather.2
  109.8 98.7 reduce-scatter.2
  212.1 50.8 all-gather.4
  431.9 97.2 reduce-scatter.4
where the time goes:
time: 547 us; the launch traced here: 538 us
  waiting for transfers between devices  250 us (46%)
  local copies, waits for them, and re-layouts  114 us (21%)
  other arithmetic  78.1 us (14%)
  matrix products  68 us (12%)
  between operations  14.4 us (3%)
  loops' own time  8.39 us (2%)
    reduce_scatter x1, waiting for transfers between devices, shards(): lax.psum_scatter(jnp.dot(context, output_weight, preferred_element_type=j...  98.4 us
    unnamed x35, local copies, waits for them, and re-layouts  92.6 us
    reduce_scatter x1, waiting for transfers between devices, shards(): lax.psum_scatter(term.astype(jnp.bfloat16), 'tensor', scatter_dimension=0...  91.4 us
    all_gather x1, waiting for transfers between devices, shards(): lax.all_gather(tokens, 'tensor', axis=0, tiled=True)  56.3 us
    scatter-add x1, other arithmetic, shards(): term = term.at[stream_slots].add(weighted)  26.5 us
    another operation x1, other arithmetic, slot_tables(): before = jnp.cumsum(hits, axis=0) - hits  23.3 us
    dot_general x1, matrix products, expert_apply(): jnp.einsum('secf,efd->secd', hidden, expert_down, preferred_element_type=...  21 us
    dot_general x1, matrix products, expert_apply(): jnp.einsum('secd,edf->secf', incoming, expert_up, preferred_element_type=...  11.7 us
  transfers between devices with their start and end apart: 5, of which 4 were waited for; matrix products, arithmetic and copies ran while one was open for 31% of the time, Pallas kernels for 0%

commit v1 on v0

--- a/solution.py
+++ b/solution.py
@@ -97,8 +97,11 @@
     inner = query_weight.shape[1]
     head_count = inner // HD
     projection = jnp.concatenate([query_weight, key_weight, value_weight], axis=1)
+    apply_fields = lambda w_in: jnp.concatenate(
+        lax.all_to_all(jnp.stack([w_in] * lax.psum(1, "tensor"), axis=0), "tensor", 0, 0), 0
+    )
     projected = jnp.dot(
-        rms_scale(lax.all_gather(tokens, "tensor", axis=0, tiled=True), attention_gain),
+        rms_scale(apply_fields(tokens), attention_gain),
         projection,
         preferred_element_type=jnp.float32,
     ).astype(jnp.bfloat16)

time: 547 us -> 605 us (1.11)
  waiting for transfers between devices: 250 us -> 288 us
  other arithmetic: 78.1 us -> 86.6 us
    all_to_all x0 -> x1, waiting for transfers between devices: none -> 95.3 us  [shards(): lax.all_to_all(jnp.stack([w_in] * lax.psum(1, 'tensor'), axis=0), 'tensor...]
    all_gather x1 -> x0, waiting for transfers between devices: 56.3 us -> none  [shards(): lax.all_gather(tokens, 'tensor', axis=0, tiled=True)]
    convert_element_type x1 -> x2, other arithmetic: 2.04 us -> 10.7 us  [rms_scale(): return (widened * inverse * gain).astype(jnp.bfloat16)]
    unnamed x35 -> x37, local copies, waits for them, and re-layouts: 92.6 us -> 92.1 us
  transfers between devices with their start and end apart: 5 -> 5, of which waited for: 4 -> 4; matrix products, arithmetic and copies ran while one was open for 31% -> 28% of each run, Pallas kernels for 0% -> 0%
where the time goes in v1:
time: 605 us; the launch traced here: 597 us
  waiting for transfers between devices  288 us (48%)
  local copies, waits for them, and re-layouts  119 us (20%)
  other arithmetic  86.6 us (14%)
  matrix products  69.9 us (12%)
  between operations  14.4 us (2%)
  starting transfers between devices  10.4 us (2%)
  loops' own time  8.84 us (1%)
    reduce_scatter x1, waiting for transfers between devices, shards(): lax.psum_scatter(jnp.dot(context, output_weight, preferred_element_type=j...  98.3 us
    all_to_all x1, waiting for transfers between devices, shards(): lax.all_to_all(jnp.stack([w_in] * lax.psum(1, 'tensor'), axis=0), 'tensor...  95.3 us
    unnamed x37, local copies, waits for them, and re-layouts  92.1 us
    reduce_scatter x1, waiting for transfers between devices, shards(): lax.psum_scatter(term.astype(jnp.bfloat16), 'tensor', scatter_dimension=0...  91.4 us
    scatter-add x1, other arithmetic, shards(): term = term.at[stream_slots].add(weighted)  26.5 us
    another operation x1, other arithmetic, slot_tables(): before = jnp.cumsum(hits, axis=0) - hits  23.3 us
    dot_general x1, matrix products, expert_apply(): jnp.einsum('secf,efd->secd', hidden, expert_down, preferred_element_type=...  21 us
  transfers between devices with their start and end apart: 5, of which 4 were waited for; matrix products, arithmetic and copies ran while one was open for 28% of the time, Pallas kernels for 0%

profile of v1, /device:TPU:0, one launch (start us, length us, event | category | flops | bytes accessed | tf_op | source)
XLA Modules:
  0.0 597.1 jit_solution(14358364524825097592)
XLA Ops:
  7.2 5.4 stack.8
  12.6 5.6 all-to-all-start
  18.3 95.3 %all-to-all-done = bf16[16,128,2048]{2,1,0:T(8,128)(2,1)} async-done(((bf16[16,128,2048]{2,1,0:T(8,128)(2,1)}), bf16[16,128,2048]{2,1,0:T(8,128)(2,1)}, u32[]{:S(2)}, u32[]{:S(2)}) %all-to-all-start) | async-done | bytes 8388640 | tf_op jit(solution)/shard_map/all_to_all | solution.py:101
  113.6 5.1 multiply_reduce_fusion
  118.7 8.7 %fusion.14 = bf16[2048,2048]{1,0:T(8,128)(2,1)} fusion(f32[2048]{0:T(1024)S(1)} %copy-done.7, f32[2048]{0:T(1024)S(1)} %rsqrt_bitcast_fusion, bf16[16,128,2048]{2,1,0:T(8,128)(2,1)} %all-to-all-done), kind=kLoop, calls=%fused_computation.24 | loop fusion | flops 16777216 | bytes 16793600 | tf_op jit(solution)/shard_map/convert_element_type | solution.py:14
  127.4 7.9 %convolution_convert_fusion.1 = bf16[2048,384]{1,0:T(8,128)(2,1)S(1)} fusion(bf16[2048,2048]{1,0:T(8,128)(2,1)} %fusion.14, bf16[2048,128]{1,0:T(8,128)(2,1)S(1)} %copy-done.12, bf16[2048,128]{1,0:T(8,128)(2,1)S(1)} %copy-done.13, bf16[2048,128]{1,0:T(8,128)(2,1)S(1)} %copy-done.14), kind=kOutput, calls=%fused_computation.47 | convolution fusion | flops 3226730496 | bytes 11534336 | tf_op jit(solution)/shard_map/dot_general | solution.py:103
  135.3 1.2 fusion.69
  136.5 26.2 %while.11 = (s32[]{:T(128)}, bf16[4,512,1,128]{3,1,2,0:T(8,128)(2,1)S(1)}, s32[4]{0:T(128)S(1)}, s32[2048]{0:T(1024)S(1)}, bf16[2048,1,128]{2,0,1:T(8,128)(2,1)S...) while((s32[]{:T(128)}, ...), condition=%wide.region_4.5_spmd.clone, body=%wide.region_1.4_spmd.clone.sunk | while | flops 548470272 | bytes 13922475 | solution.py:45
  139.7 0.7 iota_add_fusion.2
  140.4 1.3 fusion.82
  141.7 0.7 fusion.83
  142.4 0.9 fusion.84
  146.9 1.3 fusion.82
  148.1 0.7 fusion.83
  148.9 0.9 fusion.84
  152.6 0.7 iota_add_fusion.2
  153.3 1.3 fusion.82
  154.6 0.7 fusion.83
  155.3 0.9 fusion.84
  159.8 1.3 fusion.82
  161.0 0.7 fusion.83
  161.7 0.9 fusion.84
  162.7 6.6 %convolution_convert_fusion = bf16[2048,2048]{1,0:T(8,128)(2,1)} fusion(bf16[2048,128]{1,0:T(8,128)(2,1)S(1)} %bitcast.153, bf16[128,2048]{1,0:T(8,128)(2,1)} %param.25), kind=kOutput, calls=%fused_computation.28 | convolution fusion | flops 1077936128 | bytes 9437184 | tf_op jit(solution)/shard_map/dot_general | solution.py:112
  169.4 98.3 %reduce-scatter.3.cloned.1.call-done = bf16[128,2048]{1,0:T(8,128)(2,1)} async-done(((bf16[2048,2048]{1,0:T(8,128)(2,1)}), bf16[128,2048]{1,0:T(8,128)(2,1)}) %reduce-scatter.3.cloned.1.call-update) | async-done | bytes 524304 | tf_op jit(solution)/shard_map/reduce_scatter | solution.py:111
  267.7 1.3 fusion.53
  269.0 2.0 fusion.55
  271.8 1.3 copy.41
  273.2 1.7 mul.117
  274.9 23.3 %fusion.70 = s32[16,128,16]{2,0,1:T(8,128)S(1)} fusion(s32[16,128,16]{2,0,1:T(8,128)S(1)} %copy.43), kind=kOutput, calls=%fused_computation.103 | output fusion | flops 4161536 | bytes 262144 | tf_op jit(solution)/shard_map/vmap(jit(cumsum))/reduce_window_sum | solution.py:54
  298.2 1.1 sub.16
  299.3 1.6 copy.45
  301.8 45.4 %scatter_custom_fusion.2 = s32[16384]{0:T(1024)S(1)} fusion(s32[12288]{0:T(1024)S(1)} %reshape.290, s32[12288]{0:T(1024)S(1)} %reshape.292, s32[]{:T(128)} %constant.27.clone.1), kind=kCustom, calls=%fused_computation.80 | custom fusion | bytes 65540
  347.5 6.1 %gather_fusion = bf16[1024,2048]{1,0:T(8,128)(2,1)} fusion(bf16[128,2048]{1,0:T(8,128)(2,1)S(1)} %copy-done.1, s32[1024]{0:T(1024)S(1)} %broadcast_clamp_fusion), kind=kCustom, calls=%fused_computation | custom fusion | bytes 8392704 | tf_op jit(solution)/shard_map/gather | solution.py:148
  353.5 4.7 all-to-all-start.1
  358.8 0.7 reshape.298
  359.5 45.6 %scatter_custom_fusion.3 = f32[16384]{0:T(1024)S(1)} fusion(s32[12288]{0:T(1024)S(1)} %reshape.290, f32[12288]{0:T(1024)S(1)} %reshape.298, f32[]{:T(128)} %constant.9.clone.1), kind=kCustom, calls=%fused_computation.78 | custom fusion | bytes 65540
  405.3 3.3 all-to-all-done.1
  408.6 11.7 %fusion.19 = f32[16,64,1408]{2,1,0:T(8,128)} fusion(bf16[1,2048,1408]{2,1,0:T(8,128)(2,1)} %param.31, bf16[16,1,64,2048]{3,2,1,0:T(8,128)(2,1)} %all-to-all-done.1), kind=kOutput, calls=%fused_computation.33 | convolution fusion | flops 5905580032 | bytes 15728640 | tf_op jit(solution)/shard_map/secd,edf->secf/dot_general | solution.py:69
  420.3 21.0 %fusion.31 = bf16[16,64,2048]{2,1,0:T(8,128)(2,1)} fusion(bf16[1,1408,2048]{2,1,0:T(8,128)(2,1)} %param.32, f32[16,64,1408]{2,1,0:T(8,128)} %fusion.19, bf16[1,2048,1408]{2,1,0:T(8,128)(2,1)} %param.30, bf16[16,1,64,2048]{3,2,1,0:T(8,128)(2,1)} %all-to-all-done.1), kind=kOutput, calls=%fused_computation.45 | convolution fusion | flops 11821907968 | bytes 25690112 | tf_op jit(solution)/shard_map/secf,efd->secd/dot_general | solution.py:71
  441.3 5.8 fusion.49
  447.1 8.1 %fusion.57 = f32[2048,2048]{1,0:T(8,128)} fusion(bf16[176,2048]{1,0:T(8,128)(2,1)S(1)} %copy-done, f32[2048,352]{0,1:T(8,128)S(1)} %fusion.49), kind=kOutput, calls=%fused_computation.71 | convolution fusion | flops 1478557696 | bytes 20381696 | tf_op jit(solution)/shard_map/dot_general | solution.py:155
  455.2 26.5 %scatter_custom_fusion = f32[2048,2048]{1,0:T(8,128)} fusion(f32[2048,2048]{1,0:T(8,128)} %fusion.57, s32[1024]{0:T(1024)S(1)} %bitcast.157, bf16[1024,2048]{1,0:T(8,128)(2,1)} %bitcast.150, f32[1024]{0:T(1024)S(1)} %mul.121), kind=kCustom, calls=%fused_computation.27 | custom fusion | flops 6291456 | bytes 20975616 | tf_op jit(solution)/shard_map/scatter-add | solution.py:158
  481.8 9.1 %convert_element_type.109 = bf16[2048,2048]{1,0:T(8,128)(2,1)} convert(f32[2048,2048]{1,0:T(8,128)} %scatter_custom_fusion) | non-fusion elementwise | flops 4194304 | bytes 25165824 | tf_op jit(solution)/shard_map/convert_element_type | solution.py:160
  491.5 1.2 maximum_bitcast_fusion
  492.7 1.2 broadcast_in_dim.34
  493.9 3.0 scatter_fusion
  496.9 91.4 %reduce-scatter.5.cloned.1.call-done = bf16[128,2048]{1,0:T(8,128)(2,1)} async-done(((bf16[2048,2048]{1,0:T(8,128)(2,1)}), bf16[128,2048]{1,0:T(8,128)(2,1)}) %reduce-scatter.5.cloned.1.call-update) | async-done | bytes 524304 | tf_op jit(solution)/shard_map/reduce_scatter | solution.py:159
  588.3 2.1 fusion.56
  (84 shorter events, 7.8 us)
Async XLA Ops:
  7.2 439.9 %copy-start = (bf16[176,2048]{1,0:T(8,128)(2,1)S(1)}, bf16[176,2048]{1,0:T(8,128)(2,1)}, u32[]{:S(2)}) copy-start(bf16[176,2048]{1,0:T(8,128)(2,1)} %param.29) | copy-start | bytes 2162692
  12.6 101.0 %all-to-all-start = ((bf16[16,128,2048]{2,1,0:T(8,128)(2,1)}), bf16[16,128,2048]{2,1,0:T(8,128)(2,1)}, u32[]{:S(2)}, u32[]{:S(2)}) async-start(bf16[16,128,2048]{2,1,0:T(8,128)(2,1)} %stack.8), calls=%async_computation | async-start | bytes 16777216 | tf_op jit(solution)/shard_map/all_to_all | solution.py:101
  18.2 249.5 %reduce-scatter.3.cloned.1.call-start = ((), (), s32[]{:S(2)}) async-start(), calls=%async_computation.4 | async-start | bytes 8912896 | tf_op jit(solution)/shard_map/reduce_scatter | solution.py:111
  18.3 100.4 %copy-start.7 = (f32[2048]{0:T(1024)S(1)}, f32[2048]{0:T(1024)}, u32[]{:S(2)}) copy-start(f32[2048]{0:T(1024)} %param.21) | copy-start | bytes 24580
  118.7 8.7 %copy-start.12 = (bf16[2048,128]{1,0:T(8,128)(2,1)S(1)}, bf16[2048,128]{1,0:T(8,128)(2,1)}, u32[]{:S(2)}) copy-start(bf16[2048,128]{1,0:T(8,128)(2,1)} %param.24) | copy-start | bytes 1572868
  118.7 8.7 %copy-start.13 = (bf16[2048,128]{1,0:T(8,128)(2,1)S(1)}, bf16[2048,128]{1,0:T(8,128)(2,1)}, u32[]{:S(2)}) copy-start(bf16[2048,128]{1,0:T(8,128)(2,1)} %param.23) | copy-start | bytes 1572868
  118.7 8.7 %copy-start.14 = (bf16[2048,128]{1,0:T(8,128)(2,1)S(1)}, bf16[2048,128]{1,0:T(8,128)(2,1)}, u32[]{:S(2)}) copy-start(bf16[2048,128]{1,0:T(8,128)(2,1)} %param.22) | copy-start | bytes 1572868
  135.3 1.2 copy-start.6
  169.3 98.4 %copy-start.2 = (bf16[128,2048]{1,0:T(8,128)(2,1)S(1)}, bf16[128,2048]{1,0:T(8,128)(2,1)}, u32[]{:S(2)}) copy-start(bf16[128,2048]{1,0:T(8,128)(2,1)} %param.19) | copy-start | bytes 1572868
  169.3 99.7 %copy-start.8 = (f32[2048]{0:T(1024)S(1)}, f32[2048]{0:T(1024)}, u32[]{:S(2)}) copy-start(f32[2048]{0:T(1024)} %param.26) | copy-start | bytes 24580
  169.3 101.9 %copy-start.4 = (s32[2048,6]{0,1:T(8,128)S(1)}, s32[2048,6]{0,1:T(8,128)}, u32[]{:S(2)}) copy-start(s32[2048,6]{0,1:T(8,128)} %param.33) | copy-start | bytes 147460
  169.3 272.0 %all-gather.2.cloned.1.call-start = ((), (), s32[]{:S(2)}) async-start(), calls=%async_computation.5 | async-start | bytes 8912896 | tf_op jit(solution)/shard_map/all_gather | solution.py:140
  274.9 26.8 %copy-start.10 = (s32[2]{0:T(128)S(1)}, s32[2]{0:T(128)}, u32[]{:S(2)}) copy-start(s32[2]{0:T(128)} %constant.41) | copy-start | bytes 28
  274.9 26.8 %copy-start.9 = (s32[2]{0:T(128)S(1)}, s32[2]{0:T(128)}, u32[]{:S(2)}) copy-start(s32[2]{0:T(128)} %constant.69) | copy-start | bytes 28
  298.2 49.3 %copy-start.1 = (bf16[128,2048]{1,0:T(8,128)(2,1)S(1)}, bf16[128,2048]{1,0:T(8,128)(2,1)}, u32[]{:S(2)}) copy-start(bf16[128,2048]{1,0:T(8,128)(2,1)} %fusion.55) | copy-start | bytes 1572868
  353.5 4.9 copy-start.5
  353.5 55.0 %all-to-all-start.1 = ((bf16[16,1,64,2048]{3,2,1,0:T(8,128)(2,1)}), bf16[16,1,64,2048]{3,2,1,0:T(8,128)(2,1)}, u32[]{:S(2)}, u32[]{:S(2)}) async-start(bf16[16,1,64,2048]{3,2,1,0:T(8,128)(2,1)} %bitcast.149), calls=%async_computation.2 | async-start | bytes 8388608 | tf_op jit(solution)/shard_map/all_to_all | solution.py:150
  358.2 230.1 %reduce-scatter.5.cloned.1.call-start = ((), (), s32[]{:S(2)}) async-start(), calls=%async_computation.6 | async-start | bytes 8912896 | tf_op jit(solution)/shard_map/reduce_scatter | solution.py:159
  420.3 21.0 %copy-start.11 = (bf16[2048,176]{0,1:T(8,128)(2,1)S(1)}, bf16[2048,176]{0,1:T(8,128)(2,1)}, u32[]{:S(2)}) copy-start(bf16[2048,176]{0,1:T(8,128)(2,1)} %param.28) | copy-start | bytes 2162692
  490.8 0.7 copy-start.15
  491.5 96.8 %copy-start.3 = (bf16[128,2048]{1,0:T(8,128)(2,1)S(1)}, bf16[128,2048]{1,0:T(8,128)(2,1)}, u32[]{:S(2)}) copy-start(bf16[128,2048]{1,0:T(8,128)(2,1)} %reduce-scatter.3.cloned.1.call-done) | copy-start | bytes 1572868
Sparse Core Ops, SparseCore 0:
  169.4 98.1 reduce-scatter.2
  271.2 50.8 all-gather.1
  491.0 97.2 reduce-scatter.4
